TPU v7x, 32 devices: a whole 2x2x4 slice. The times are simulated.
32 devices in a mesh: dp: 8 (over y, x, core), space: 4 (over z).
Axes of the slice: x: 2, y: 2, z: 4, core: 2. Of those that a mesh axis runs over, the one named last changes fastest.
Arguments:
- latents: bfloat16 [8, 33, 4, 8, 256], P('dp', None, 'space'), may hold values from -6 to 6
- lengths: int32 [8], P('dp'), may hold values from 9 to 33, as said below
- spatial_weight: bfloat16 [3, 3, 256, 256], replicated, may hold values from -0.125 to 0.125
- temporal_weight: bfloat16 [3, 256, 256], replicated, may hold values from -0.21875 to 0.21875
- critic_weight: bfloat16 [256, 256], replicated, may hold values from -0.375 to 0.375
- critic_head: float32 [256], replicated, may hold values from -5 to 5
- critic_frames: int32 [8, 8], P('dp'), may hold values from 0 to 32, as said below
- recon_grad: bfloat16 [8, 33, 8, 16, 256], P('dp', None, 'space'), may hold values from -6 to 6
Outputs:
- decoded: bfloat16 [8, 33, 8, 16, 256], P('dp', None, 'space')
- grad_spatial: float32 [589824], P(('dp', 'space'))
- grad_temporal: float32 [196608], P(('dp', 'space'))
Inputs may be any that keep to these rules, and one draw needn't show every extreme that they name: `lengths`: some clip has exactly 33 live frames and some exactly 9. `critic_frames`: each entry names a live frame of its clip (below that clip's length); a frame may be named by several slots.
All inputs are finite; a program needn't handle non-finite values.
Results may differ from a plain program's by a relative error of at most 0.0055.
Values may be sent and summed in bfloat16 or wider, within the bound.
No kernel may reach another device: no remote copies, remote signals or barrier semaphores. Data moves between devices by JAX's collectives and lax.ppermute only.
A program may use at most 64 MiB of HBM per device.

v0:
```python
import math

import jax
import jax.numpy as jnp
from jax import lax
from jax.sharding import PartitionSpec as P


def extended_2(cells, sides, width):
    for axis, dim in sides:
        count = lax.axis_size(axis)
        ends = count - 1
        head = lax.slice_in_dim(cells, 0, width, axis=dim)
        tail = lax.slice_in_dim(cells, cells.shape[dim] - width, cells.shape[dim], axis=dim)
        cells = jnp.concatenate(
            [
                lax.ppermute(tail, axis, [(i, (i + 1) % count) for i in range(ends)]),
                cells,
                lax.ppermute(head, axis, [((i + 1) % count, i) for i in range(ends)]),
            ],
            axis=dim,
        )
    return cells


def upsample(values):
    doubled = jnp.repeat(values, 2, axis=-3)
    return jnp.repeat(doubled, 2, axis=-2)


def silu_slope(pre_act):
    sigmoid_val = jax.nn.sigmoid(pre_act)
    return sigmoid_val * (1.0 + pre_act * (1.0 - sigmoid_val))


def delayed(values, offset):
    if offset == 0:
        return values
    widths = [(0, 0)] * values.ndim
    widths[1] = (offset, 0)
    return jnp.pad(values, widths)[:, : values.shape[1]]


def advanced(values, offset):
    if offset == 0:
        return values
    widths = [(0, 0)] * values.ndim
    widths[1] = (0, offset)
    return jnp.pad(values, widths)[:, offset:]


def critic_slope(hidden, feature, critic_weight, critic_head):
    score_val = jnp.sum(feature * critic_head, axis=-1)
    factor = -jax.nn.sigmoid(-score_val)[..., None] * critic_head
    unused, pullback = jax.vjp(jax.nn.gelu, hidden)
    gelu_slope = pullback(jnp.broadcast_to(factor[..., None, None, :], hidden.shape))[0].astype(
        jnp.bfloat16
    )
    return jnp.einsum(
        "nqhwe,ce->nqhwc", gelu_slope, critic_weight, preferred_element_type=jnp.float32
    )


def on_device(
    latents,
    lengths,
    spatial_weight,
    temporal_weight,
    critic_weight,
    critic_head,
    critic_frames,
    recon_grad,
):
    groups = lax.axis_size("space")
    clip_count = latents.shape[0] * lax.axis_size("dp")
    frame_count = latents.shape[1]
    upsampled = upsample(latents)
    extended = extended_2(upsampled, (("space", 2),), 1)
    padded = jnp.pad(extended, ((0, 0), (0, 0), (0, 0), (1, 1), (0, 0)))
    height = upsampled.shape[2]
    width = upsampled.shape[3]
    pre_act = jnp.zeros(upsampled.shape, jnp.float32)
    for row_tap in range(3):
        for col_tap in range(3):
            window = padded[:, :, row_tap : row_tap + height, col_tap : col_tap + width]
            pre_act = pre_act + jnp.einsum(
                "nfhwc,cd->nfhwd",
                window,
                spatial_weight[row_tap, col_tap],
                preferred_element_type=jnp.float32,
            )
    activated = jax.nn.silu(pre_act).astype(jnp.bfloat16)
    mixing = jnp.zeros(upsampled.shape, jnp.float32)
    for offset in range(3):
        mixing = mixing + jnp.einsum(
            "nfhwc,cd->nfhwd",
            delayed(activated, offset),
            temporal_weight[offset],
            preferred_element_type=jnp.float32,
        )
    alive_mask = (jnp.arange(frame_count)[None, :] < lengths[:, None]).astype(jnp.float32)[
        :, :, None, None, None
    ]
    decoded = (alive_mask * (upsampled.astype(jnp.float32) + mixing)).astype(jnp.bfloat16)
    chosen = jax.vmap(lambda clip_frames, indices: jnp.take(clip_frames, indices, axis=0))(
        decoded, critic_frames
    )
    hidden = jnp.einsum(
        "nqhwc,ce->nqhwe",
        lax.all_to_all(chosen, "space", split_axis=1, concat_axis=2, tiled=True),
        critic_weight,
        preferred_element_type=jnp.float32,
    )
    feature = jnp.mean(jax.nn.gelu(hidden), axis=(2, 3))
    slope_rows = critic_slope(hidden, feature, critic_weight, critic_head)
    adverse = lax.all_to_all(
        slope_rows.astype(jnp.bfloat16), "space", split_axis=2, concat_axis=1, tiled=True
    ).astype(slope_rows.dtype)
    selector = (critic_frames[:, :, None] == jnp.arange(frame_count)[None, None, :]).astype(
        jnp.float32
    )
    adverse_frames = jnp.einsum(
        "nqf,nqhwc->nfhwc", selector, adverse, precision=lax.Precision.HIGHEST
    )
    loss_scale = 1.0 / math.sqrt(clip_count * frame_count * height * groups * width)
    cotangent = (
        alive_mask * loss_scale * (recon_grad.astype(jnp.float32) + adverse_frames)
    ).astype(jnp.bfloat16)
    temporal_grad = jnp.stack(
        [
            jnp.einsum(
                "nfhwc,nfhwd->cd",
                delayed(activated, offset),
                cotangent,
                preferred_element_type=jnp.float32,
            )
            for offset in range(3)
        ]
    ).reshape(-1)
    act_grad = jnp.zeros(upsampled.shape, jnp.float32)
    for offset in range(3):
        act_grad = act_grad + jnp.einsum(
            "nfhwd,cd->nfhwc",
            advanced(cotangent, offset),
            temporal_weight[offset],
            preferred_element_type=jnp.float32,
        )
    pre_slope = (act_grad * silu_slope(pre_act)).astype(jnp.bfloat16)
    tap_grads = []
    for row_tap in range(3):
        for col_tap in range(3):
            window = padded[:, :, row_tap : row_tap + height, col_tap : col_tap + width]
            tap_grads.append(
                jnp.einsum("nfhwc,nfhwd->cd", window, pre_slope, preferred_element_type=jnp.float32)
            )
    spatial_share = lax.psum_scatter(
        jnp.stack(tap_grads).reshape(-1), ("dp", "space"), scatter_dimension=0, tiled=True
    )
    temporal_share = lax.psum_scatter(
        temporal_grad, ("dp", "space"), scatter_dimension=0, tiled=True
    )
    return (decoded, spatial_share, temporal_share)


def solution(mesh):
    placed = (
        P("dp", None, "space", None, None),
        P("dp"),
        P(),
        P(),
        P(),
        P(),
        P("dp", None),
        P("dp", None, "space", None, None),
    )
    return jax.shard_map(
        on_device,
        mesh=mesh,
        in_specs=placed,
        out_specs=(P("dp", None, "space", None, None), P(("dp", "space")), P(("dp", "space"))),
        check_vma=False,
    )
```

profile of v0, /device:TPU:0, one launch (start us, length us, event | category | flops | bytes accessed | tf_op | source)
XLA Modules:
  0.0 220.8 jit_solution(4576790732712989588)
XLA Ops:
  7.2 1.1 broadcast_in_dim.38
  8.4 5.0 %collective-permute-start = (bf16[1,33,1,16,256]{4,3,2,1,0:T(8,128)(2,1)S(1)}, bf16[1,33,1,16,256]{4,3,2,1,0:T(8,128)(2,1)S(1)}, u32[]{:S(2)}, u32[]{:S(2)}) collective-permute-start(bf16[1,33,1,16,256]{4,3,2,1,0:T(8,128)(2,1)S(1)} %slice.96), channel_id=1, source_target_pairs={{0,1},{1,2},{2,3},{4,5},{5,6},{6,7},{8,9},{9,10},{10,11},{12,13},{... | collective-permute-start | bytes 811016 | tf_op jit(solution)/shard_map/ppermute | solution.py:17
  13.4 1.3 collective-permute-start.1
  14.7 0.7 fusion.127
  15.3 0.7 and_bitcast_fusion
  16.8 1.2 fusion.50
  18.0 1.0 collective-permute-done
  19.1 4.1 %collective-permute-done.1 = bf16[1,33,1,16,256]{4,3,2,1,0:T(8,128)(2,1)S(1)} collective-permute-done((bf16[1,33,1,16,256]{4,3,2,1,0:T(8,128)(2,1)S(1)}, bf16[1,33,1,16,256]{4,3,2,1,0:T(8,128)(2,1)S(1)}, u32[]{:S(2)}, u32[]{:S(2)}) %collective-permute-start.1) | collective-permute-done | bytes 270368 | tf_op jit(solution)/shard_map/ppermute | solution.py:19
  23.3 0.9 fusion.5
  24.2 0.4 copy-done.1
  25.8 0.3 fusion.44
  26.8 1.7 multiply_convert_fusion
  29.1 1.1 fusion.17
  30.2 2.3 %gather_fusion = bf16[8,2,16,256]{3,2,1,0:T(8,128)(2,1)} fusion(bf16[1,33,2,16,256]{4,3,2,1,0:T(8,128)(2,1)} %fusion.17, s32[8]{0:T(128)S(1)} %or_bitcast_fusion), kind=kCustom, calls=%fused_computation | custom fusion | bytes 262208 | tf_op jit(solution)/shard_map/vmap(jit(_take))/gather | solution.py:105
  32.5 1.6 fusion.86
  34.1 4.0 %all-to-all-start = ((bf16[1,8,2,16,256]{4,3,2,0,1:T(8,128)(2,1)}), bf16[1,8,2,16,256]{4,3,2,0,1:T(8,128)(2,1)}, u32[]{:S(2)}, u32[]{:S(2)}) async-start(bf16[1,8,2,16,256]{4,3,2,0,1:T(8,128)(2,1)} %fusion.86), calls=%async_computation | async-start | bytes 262144 | tf_op jit(solution)/shard_map/all_to_all | solution.py:110
  38.1 6.0 %all-to-all-done = bf16[1,8,2,16,256]{4,3,2,0,1:T(8,128)(2,1)} async-done(((bf16[1,8,2,16,256]{4,3,2,0,1:T(8,128)(2,1)}), bf16[1,8,2,16,256]{4,3,2,0,1:T(8,128)(2,1)}, u32[]{:S(2)}, u32[]{:S(2)}) %all-to-all-start) | async-done | bytes 131104 | tf_op jit(solution)/shard_map/all_to_all | solution.py:110
  44.1 0.9 copy.73
  45.8 0.7 copy.74
  46.5 4.0 %all-to-all-start.1 = ((bf16[1,2,8,16,256]{4,3,1,0,2:T(8,128)(2,1)}), bf16[1,2,8,16,256]{4,3,1,0,2:T(8,128)(2,1)}, u32[]{:S(2)}, u32[]{:S(2)}) async-start(bf16[1,2,8,16,256]{4,3,1,0,2:T(8,128)(2,1)} %copy.74), calls=%async_computation.1 | async-start | bytes 262144 | tf_op jit(solution)/shard_map/all_to_all | solution.py:116
  50.7 5.7 %all-to-all-done.1 = bf16[1,2,8,16,256]{4,3,1,0,2:T(8,128)(2,1)} async-done(((bf16[1,2,8,16,256]{4,3,1,0,2:T(8,128)(2,1)}), bf16[1,2,8,16,256]{4,3,1,0,2:T(8,128)(2,1)}, u32[]{:S(2)}, u32[]{:S(2)}) %all-to-all-start.1) | async-done | bytes 131104 | tf_op jit(solution)/shard_map/all_to_all | solution.py:116
  56.4 1.7 copy.126
  58.1 1.6 reshape.350
  59.7 1.7 fusion.14
  61.4 0.4 convolution_bitcast_fusion.1
  61.8 0.4 convolution_bitcast_fusion.2
  62.1 0.4 convolution_bitcast_fusion.3
  62.5 0.4 slice_bitcast_fusion
  62.9 0.3 fusion.64
  63.3 1.3 copy.111
  64.7 0.3 convolution_add_fusion.1
  65.0 0.9 copy-done.3
  65.9 0.6 fusion.15
  66.5 0.4 fusion.26
  66.9 0.6 copy-done.7
  67.4 0.4 fusion.25
  67.8 0.4 fusion.24
  68.3 0.4 fusion.23
  68.6 0.4 fusion.22
  69.0 0.4 fusion.21
  69.4 0.4 fusion.20
  69.8 0.6 copy-done.5
  70.4 0.4 fusion.19
  70.8 0.4 fusion.18
  71.2 2.6 %copy.110 = f32[288,2,8,128]{3,1,2,0:T(2,128)} copy(f32[288,2,8,128]{3,2,1,0:T(8,128)S(1)} %bitcast.315) | data formatting | bytes 4718592
  73.9 137.3 %all-reduce.10.cloned.1.call-done = (f32[589824]{0:T(1024)}, f32[196608]{0:T(1024)}) async-done(((f32[589824]{0:T(1024)}, f32[196608]{0:T(1024)}), (f32[589824]{0:T(1024)}, f32[196608]{0:T(1024)})) %all-reduce.10.cloned.1.call-update) | async-done | bytes 3145744
  211.1 1.5 dynamic-slice
  212.6 1.3 dynamic-slice.1
  (41 shorter events, 3.9 us)
Async XLA Ops:
  7.2 37.8 %copy-start = (bf16[256,256]{1,0:T(8,128)(2,1)S(1)}, bf16[256,256]{1,0:T(8,128)(2,1)}, u32[]{:S(2)}) copy-start(bf16[256,256]{1,0:T(8,128)(2,1)} %param.12) | copy-start | bytes 393220
  8.4 10.7 %collective-permute-start = (bf16[1,33,1,16,256]{4,3,2,1,0:T(8,128)(2,1)S(1)}, bf16[1,33,1,16,256]{4,3,2,1,0:T(8,128)(2,1)S(1)}, u32[]{:S(2)}, u32[]{:S(2)}) collective-permute-start(bf16[1,33,1,16,256]{4,3,2,1,0:T(8,128)(2,1)S(1)} %slice.96), channel_id=1, source_target_pairs={{0,1},{1,2},{2,3},{4,5},{5,6},{6,7},{8,9},{9,10},{10,11},{12,13},{... | collective-permute-start | bytes 811016 | tf_op jit(solution)/shard_map/ppermute | solution.py:17
  13.4 9.8 %collective-permute-start.1 = (bf16[1,33,1,16,256]{4,3,2,1,0:T(8,128)(2,1)S(1)}, bf16[1,33,1,16,256]{4,3,2,1,0:T(8,128)(2,1)S(1)}, u32[]{:S(2)}, u32[]{:S(2)}) collective-permute-start(bf16[1,33,1,16,256]{4,3,2,1,0:T(8,128)(2,1)S(1)} %slice.96), channel_id=1, source_target_pairs={{1,0},{2,1},{3,2},{5,4},{6,5},{7,6},{9,8},{10,9},{11,10},{13,12},{... | collective-permute-start | bytes 811016 | tf_op jit(solution)/shard_map/ppermute | solution.py:19
  19.1 7.1 %copy-start.6 = (bf16[1,33,1,16,256]{4,3,2,1,0:T(8,128)(2,1)}, bf16[1,33,1,16,256]{4,3,2,1,0:T(8,128)(2,1)S(1)}, u32[]{:S(2)}) copy-start(bf16[1,33,1,16,256]{4,3,2,1,0:T(8,128)(2,1)S(1)} %collective-permute-done) | copy-start | bytes 811012
  23.2 3.3 %copy-start.4 = (bf16[1,33,1,16,256]{4,3,2,1,0:T(8,128)(2,1)}, bf16[1,33,1,16,256]{4,3,2,1,0:T(8,128)(2,1)S(1)}, u32[]{:S(2)}) copy-start(bf16[1,33,1,16,256]{4,3,2,1,0:T(8,128)(2,1)S(1)} %collective-permute-done.1) | copy-start | bytes 811012
  23.2 1.3 copy-start.1
  26.8 1.7 copy-start.2
  29.1 9.0 %copy-start.8 = (f32[256]{0:T(256)S(1)}, f32[256]{0:T(256)}, u32[]{:S(2)}) copy-start(f32[256]{0:T(256)} %param.13) | copy-start | bytes 3076
  34.1 9.9 %all-to-all-start = ((bf16[1,8,2,16,256]{4,3,2,0,1:T(8,128)(2,1)}), bf16[1,8,2,16,256]{4,3,2,0,1:T(8,128)(2,1)}, u32[]{:S(2)}, u32[]{:S(2)}) async-start(bf16[1,8,2,16,256]{4,3,2,0,1:T(8,128)(2,1)} %fusion.86), calls=%async_computation | async-start | bytes 262144 | tf_op jit(solution)/shard_map/all_to_all | solution.py:110
  45.5 14.2 %copy-start.9 = (s32[1,8]{1,0:T(1,128)S(1)}, s32[1,8]{1,0:T(1,128)}, u32[]{:S(2)}) copy-start(s32[1,8]{1,0:T(1,128)} %param.14) | copy-start | bytes 100
  46.5 9.9 %all-to-all-start.1 = ((bf16[1,2,8,16,256]{4,3,1,0,2:T(8,128)(2,1)}), bf16[1,2,8,16,256]{4,3,1,0,2:T(8,128)(2,1)}, u32[]{:S(2)}, u32[]{:S(2)}) async-start(bf16[1,2,8,16,256]{4,3,1,0,2:T(8,128)(2,1)} %copy.74), calls=%async_computation.1 | async-start | bytes 262144 | tf_op jit(solution)/shard_map/all_to_all | solution.py:116
  50.4 160.7 %all-reduce.10.cloned.1.call-start = ((), (), s32[]{:S(2)}) async-start(), calls=%async_computation.2 | async-start | bytes 6291456
  64.7 1.2 copy-start.3
  66.5 1.0 copy-start.7
  69.4 1.0 copy-start.5
Sparse Core Ops, SparseCore 0:
  74.0 137.0 all-reduce.9
where the time goes:
time: 222 us; the launch traced here: 221 us
  waiting for transfers between devices  154 us (69%)
  local copies, waits for them, and re-layouts  18.2 us (8%)
  between operations  15 us (7%)
  matrix products  14.9 us (7%)
  starting transfers between devices  14.4 us (6%)
  other arithmetic  4.19 us (2%)
    unnamed x2, waiting for transfers between devices  137 us
    unnamed x24, local copies, waits for them, and re-layouts  9.26 us
    all_to_all x1, waiting for transfers between devices, on_device(): lax.all_to_all(chosen, 'space', split_axis=1, concat_axis=2, tiled=True)  5.96 us
    all_to_all x1, waiting for transfers between devices, on_device(): lax.all_to_all(slope_rows.astype(jnp.bfloat16), 'space', split_axis=2, co...  5.74 us
    dot_general x9, matrix products, on_device(): jnp.einsum('nfhwc,cd->nfhwd', window, spatial_weight[row_tap, col_tap], p...  5.02 us
    ppermute x1, starting transfers between devices, extended_2(): lax.ppermute(tail, axis, [(i, (i + 1) % count) for i in range(ends)])  4.97 us
  transfers between devices with their start and end apart: 5, of which 5 were waited for; matrix products, arithmetic and copies ran while one was open for 1% of the time, Pallas kernels for 0%

commit v1 on v0

--- a/solution.py
+++ b/solution.py
@@ -6,21 +6,19 @@
 from jax.sharding import PartitionSpec as P
 
 
-def extended_2(cells, sides, width):
-    for axis, dim in sides:
-        count = lax.axis_size(axis)
-        ends = count - 1
-        head = lax.slice_in_dim(cells, 0, width, axis=dim)
-        tail = lax.slice_in_dim(cells, cells.shape[dim] - width, cells.shape[dim], axis=dim)
-        cells = jnp.concatenate(
-            [
-                lax.ppermute(tail, axis, [(i, (i + 1) % count) for i in range(ends)]),
-                cells,
-                lax.ppermute(head, axis, [((i + 1) % count, i) for i in range(ends)]),
-            ],
-            axis=dim,
-        )
-    return cells
+def _log2(n):
+    b = n.bit_length() - 1
+    return b if (1 << b) == n else None
+
+
+def exchange_rows(cells, axis, dim):
+    count = lax.axis_size(axis)
+    ends = count - 1
+    head = lax.slice_in_dim(cells, 0, 1, axis=dim)
+    tail = lax.slice_in_dim(cells, cells.shape[dim] - 1, cells.shape[dim], axis=dim)
+    above = lax.ppermute(tail, axis, [(i, i + 1) for i in range(ends)])
+    below = lax.ppermute(head, axis, [(i + 1, i) for i in range(ends)])
+    return above, below
 
 
 def upsample(values):
@@ -49,16 +47,37 @@
     return jnp.pad(values, widths)[:, offset:]
 
 
-def critic_slope(hidden, feature, critic_weight, critic_head):
-    score_val = jnp.sum(feature * critic_head, axis=-1)
-    factor = -jax.nn.sigmoid(-score_val)[..., None] * critic_head
-    unused, pullback = jax.vjp(jax.nn.gelu, hidden)
-    gelu_slope = pullback(jnp.broadcast_to(factor[..., None, None, :], hidden.shape))[0].astype(
-        jnp.bfloat16
-    )
-    return jnp.einsum(
-        "nqhwe,ce->nqhwc", gelu_slope, critic_weight, preferred_element_type=jnp.float32
-    )
+def space_sum(values):
+    count = lax.axis_size("space")
+    bits = _log2(count)
+    if bits is None:
+        return lax.psum(values, "space")
+    for bit in range(bits):
+        step = 1 << bit
+        values = values + lax.ppermute(values, "space", [(i, i ^ step) for i in range(count)])
+    return values
+
+
+def halving_scatter(blocks):
+    nd, ns = lax.axis_size("dp"), lax.axis_size("space")
+    bd, bs = _log2(nd), _log2(ns)
+    if bd is None or bs is None:
+        flat = lax.psum_scatter(blocks.reshape(-1), "dp", scatter_dimension=0, tiled=True)
+        return lax.psum_scatter(flat, "space", scatter_dimension=0, tiled=True)
+    width = blocks.shape[1]
+    dims = {("dp", i): bd - 1 - i for i in range(bd)}
+    dims.update({("space", i): bd + bs - 1 - i for i in range(bs)})
+    order = [("dp", i) for i in range(bd)] + [("space", i) for i in range(bs)]
+    cur = jnp.transpose(
+        blocks.reshape([2] * (bd + bs) + [width]), [dims[st] for st in order] + [bd + bs]
+    )
+    for axis, bit in order:
+        size = nd if axis == "dp" else ns
+        mine = (lax.axis_index(axis) // (1 << bit)) % 2
+        keep = lax.dynamic_index_in_dim(cur, mine, 0, keepdims=False)
+        send = lax.dynamic_index_in_dim(cur, 1 - mine, 0, keepdims=False)
+        cur = keep + lax.ppermute(send, axis, [(i, i ^ (1 << bit)) for i in range(size)])
+    return cur
 
 
 def on_device(
@@ -72,10 +91,14 @@
     recon_grad,
 ):
     groups = lax.axis_size("space")
+    devices = lax.axis_size("dp") * groups
     clip_count = latents.shape[0] * lax.axis_size("dp")
     frame_count = latents.shape[1]
     upsampled = upsample(latents)
-    extended = extended_2(upsampled, (("space", 2),), 1)
+    above, below = exchange_rows(latents, "space", 2)
+    extended = jnp.concatenate(
+        [upsample(above)[:, :, 1:], upsampled, upsample(below)[:, :, :1]], axis=2
+    )
     padded = jnp.pad(extended, ((0, 0), (0, 0), (0, 0), (1, 1), (0, 0)))
     height = upsampled.shape[2]
     width = upsampled.shape[3]
@@ -106,21 +129,23 @@
         decoded, critic_frames
     )
     hidden = jnp.einsum(
-        "nqhwc,ce->nqhwe",
-        lax.all_to_all(chosen, "space", split_axis=1, concat_axis=2, tiled=True),
-        critic_weight,
-        preferred_element_type=jnp.float32,
-    )
-    feature = jnp.mean(jax.nn.gelu(hidden), axis=(2, 3))
-    slope_rows = critic_slope(hidden, feature, critic_weight, critic_head)
-    adverse = lax.all_to_all(
-        slope_rows.astype(jnp.bfloat16), "space", split_axis=2, concat_axis=1, tiled=True
-    ).astype(slope_rows.dtype)
+        "nqhwc,ce->nqhwe", chosen, critic_weight, preferred_element_type=jnp.float32
+    )
+    feature = space_sum(jnp.sum(jax.nn.gelu(hidden), axis=(2, 3))) / (height * groups * width)
+    score_val = jnp.sum(feature * critic_head, axis=-1)
+    factor = -jax.nn.sigmoid(-score_val)[..., None] * critic_head
+    unused, pullback = jax.vjp(jax.nn.gelu, hidden)
+    gelu_slope = pullback(jnp.broadcast_to(factor[..., None, None, :], hidden.shape))[0].astype(
+        jnp.bfloat16
+    )
+    slope_rows = jnp.einsum(
+        "nqhwe,ce->nqhwc", gelu_slope, critic_weight, preferred_element_type=jnp.float32
+    )
     selector = (critic_frames[:, :, None] == jnp.arange(frame_count)[None, None, :]).astype(
         jnp.float32
     )
     adverse_frames = jnp.einsum(
-        "nqf,nqhwc->nfhwc", selector, adverse, precision=lax.Precision.HIGHEST
+        "nqf,nqhwc->nfhwc", selector, slope_rows, precision=lax.Precision.HIGHEST
     )
     loss_scale = 1.0 / math.sqrt(clip_count * frame_count * height * groups * width)
     cotangent = (
@@ -136,7 +161,7 @@
             )
             for offset in range(3)
         ]
-    ).reshape(-1)
+    )
     act_grad = jnp.zeros(upsampled.shape, jnp.float32)
     for offset in range(3):
         act_grad = act_grad + jnp.einsum(
@@ -153,13 +178,11 @@
             tap_grads.append(
                 jnp.einsum("nfhwc,nfhwd->cd", window, pre_slope, preferred_element_type=jnp.float32)
             )
-    spatial_share = lax.psum_scatter(
-        jnp.stack(tap_grads).reshape(-1), ("dp", "space"), scatter_dimension=0, tiled=True
-    )
-    temporal_share = lax.psum_scatter(
-        temporal_grad, ("dp", "space"), scatter_dimension=0, tiled=True
-    )
-    return (decoded, spatial_share, temporal_share)
+    spatial_grad = jnp.stack(tap_grads).reshape(devices, -1)
+    temporal_grad = temporal_grad.reshape(devices, -1)
+    share = halving_scatter(jnp.concatenate([spatial_grad, temporal_grad], axis=1))
+    spatial_width = spatial_grad.shape[1]
+    return (decoded, share[:spatial_width], share[spatial_width:])
 
 
 def solution(mesh):

time: 222 us -> 115 us (0.52)
  waiting for transfers between devices: 154 us -> 43.3 us
  between operations: 15 us -> 1.68 us
  matrix products: 14.9 us -> 24.6 us
  other arithmetic: 4.19 us -> 8.67 us
  starting transfers between devices: 14.4 us -> 17.9 us
    unnamed x2 -> x0, waiting for transfers between devices: 137 us -> none
    ppermute x2 -> x9, waiting for transfers between devices: 5.15 us -> 43.3 us  [the longest x5 37.7 us: halving_scatter(): lax.ppermute(send, axis, [(i, i ^ 1 << bit) for i in range(size)])]
    all_to_all x2 -> x0, waiting for transfers between devices: 11.7 us -> none  [the longest x1 5.96 us: on_device(): lax.all_to_all(chosen, 'space', split_axis=1, concat_axis=2, tiled=True)]
    ppermute x2 -> x9, starting transfers between devices: 6.26 us -> 17.9 us  [the longest x5 7.37 us: halving_scatter(): lax.ppermute(send, axis, [(i, i ^ 1 << bit) for i in range(size)])]
    all_to_all x2 -> x0, starting transfers between devices: 7.91 us -> none  [the longest x1 3.95 us: on_device(): lax.all_to_all(slope_rows.astype(jnp.bfloat16), 'space', split_axis=2, co...]
    dot_general x9, matrix products: 3.52 us -> 10.1 us  [on_device(): jnp.einsum('nfhwc,nfhwd->cd', window, pre_slope, preferred_element_type=j...]
    concatenate x0 -> x3, local copies, waits for them, and re-layouts: none -> 5.57 us  [on_device(): jnp.concatenate([spatial_grad, temporal_grad], axis=1)]
    unnamed x24 -> x32, local copies, waits for them, and re-layouts: 9.26 us -> 4.5 us
  transfers between devices with their start and end apart: 5 -> 9, of which waited for: 5 -> 8; matrix products, arithmetic and copies ran while one was open for 1% -> 3% of each run, Pallas kernels for 0% -> 0%
where the time goes in v1:
time: 115 us
  waiting for transfers between devices  43.3 us (38%)
  matrix products  24.6 us (21%)
  local copies, waits for them, and re-layouts  18.7 us (16%)
  starting transfers between devices  17.9 us (16%)
  other arithmetic  8.67 us (8%)
  between operations  1.68 us (1%)
    ppermute x5, waiting for transfers between devices, halving_scatter(): lax.ppermute(send, axis, [(i, i ^ 1 << bit) for i in range(size)])  37.7 us
    dot_general x9, matrix products, on_device(): jnp.einsum('nfhwc,nfhwd->cd', window, pre_slope, preferred_element_type=j...  10.1 us
    ppermute x5, starting transfers between devices, halving_scatter(): lax.ppermute(send, axis, [(i, i ^ 1 << bit) for i in range(size)])  7.37 us
    concatenate x3, local copies, waits for them, and re-layouts, on_device(): jnp.concatenate([spatial_grad, temporal_grad], axis=1)  5.57 us
    ppermute x1, starting transfers between devices, exchange_rows(): above = lax.ppermute(tail, axis, [(i, i + 1) for i in range(ends)])  5.1 us
    dot_general x3, matrix products, on_device(): jnp.einsum('nfhwd,cd->nfhwc', advanced(cotangent, offset), temporal_weigh...  4.77 us
    unnamed x32, local copies, waits for them, and re-layouts  4.5 us
    add x5, other arithmetic, halving_scatter(): keep + lax.ppermute(send, axis, [(i, i ^ 1 << bit) for i in range(size)])  4.18 us
  transfers between devices with their start and end apart: 9, of which 8 were waited for; matrix products, arithmetic and copies ran while one was open for 3% of the time, Pallas kernels for 0%

profile of v1, /device:TPU:0, one launch (start us, length us, event | category | flops | bytes accessed | tf_op | source)
XLA Modules:
  0.0 114.9 jit_solution(12019754456863461973)
XLA Ops:
  0.6 5.1 %collective-permute-start = (bf16[1,33,1,8,256]{4,3,2,1,0:T(8,128)(2,1)}, bf16[1,33,1,8,256]{4,3,2,1,0:T(8,128)(2,1)S(1)}, u32[]{:S(2)}, u32[]{:S(2)}) collective-permute-start(bf16[1,33,1,8,256]{4,3,2,1,0:T(8,128)(2,1)} %param.8), channel_id=1, source_target_pairs={{0,1},{1,2},{2,3},{4,5},{5,6},{6,7},{8,9},{9,10},{10,11},{12,13},{... | collective-permute-start | bytes 405512 | tf_op jit(solution)/shard_map/ppermute | solution.py:19
  5.8 1.3 %collective-permute-start.1 = (bf16[1,33,1,8,256]{4,3,2,1,0:T(8,128)(2,1)}, bf16[1,33,1,8,256]{4,3,2,1,0:T(8,128)(2,1)S(1)}, u32[]{:S(2)}, u32[]{:S(2)}) collective-permute-start(bf16[1,33,1,8,256]{4,3,2,1,0:T(8,128)(2,1)} %param.8), channel_id=1, source_target_pairs={{1,0},{2,1},{3,2},{5,4},{6,5},{7,6},{9,8},{10,9},{11,10},{13,12},{... | collective-permute-start | bytes 405512 | tf_op jit(solution)/shard_map/ppermute | solution.py:20
  7.1 0.7 fusion.106
  7.7 0.7 and_bitcast_fusion
  8.4 1.0 broadcast_in_dim.46
  9.6 0.9 convert_element_type.56
  11.4 1.5 %collective-permute-done.1 = bf16[1,33,1,8,256]{4,3,2,1,0:T(8,128)(2,1)S(1)} collective-permute-done((bf16[1,33,1,8,256]{4,3,2,1,0:T(8,128)(2,1)}, bf16[1,33,1,8,256]{4,3,2,1,0:T(8,128)(2,1)S(1)}, u32[]{:S(2)}, u32[]{:S(2)}) %collective-permute-start.1) | collective-permute-done | bytes 135200 | tf_op jit(solution)/shard_map/ppermute | solution.py:20
  13.2 0.9 fusion.5
  17.1 1.4 %multiply_convert_fusion = (bf16[33,2,16,256]{3,2,1,0:T(8,128)(2,1)S(1)}, f32[33,2,16,256]{3,2,1,0:T(8,128)}) fusion(f32[33,2,16,256]{3,2,1,0:T(8,128)S(1)} %convolution_add_fusion.5, bf16[3,3,256,256]{3,2,1,0:T(8,128)(2,1)S(1)} %copy-done.9, bf16[1,33,4,18,256]{4,3,2,1,0:T(8,128)(2,1)S(1)} %fusion.5), kind=kOutput, calls=%fused_computation.54 | convolution fusion | flops 140034048 | bytes 3375104 | tf_op jit(solution)/shard_map/nfhwc,cd->nfhwd/dot_general | solution.py:109
  19.1 0.7 copy-done.7
  19.9 1.1 fusion.14
  21.0 2.3 %gather_fusion = bf16[8,2,16,256]{3,2,1,0:T(8,128)(2,1)} fusion(bf16[1,33,2,16,256]{4,3,2,1,0:T(8,128)(2,1)} %fusion.14, s32[8]{0:T(128)S(1)} %or_bitcast_fusion), kind=kCustom, calls=%fused_computation | custom fusion | bytes 262208 | tf_op jit(solution)/shard_map/vmap(jit(_take))/gather | solution.py:128
  23.2 1.8 %fusion.49 = (f32[8,256]{1,0:T(8,128)S(1)}, f32[8,2,16,256]{3,2,1,0:T(8,128)}) fusion(bf16[256,256]{1,0:T(8,128)(2,1)S(1)} %copy-done, bf16[8,2,16,256]{3,2,1,0:T(8,128)(2,1)} %gather_fusion, pred[8]{0:T(512)(128)(4,1)S(1)} %and_bitcast_fusion), kind=kOutput, calls=%fused_computation.93 | convolution fusion | flops 34207744 | bytes 532488 | tf_op jit(solution)/shard_map/nqhwc,ce->nqhwe/dot_general | solution.py:131
  25.1 1.6 %collective-permute-start.2 = (f32[1,8,256]{2,1,0:T(8,128)S(1)}, f32[1,8,256]{2,1,0:T(8,128)S(1)}, u32[]{:S(2)}, u32[]{:S(2)}) collective-permute-start(f32[1,8,256]{2,1,0:T(8,128)S(1)} %bitcast.322), channel_id=1, source_target_pairs={{0,1},{1,0},{2,3},{3,2},{4,5},{5,4},{6,7},{7,6},{8,9},{9,8},{10,11... | collective-permute-start | bytes 24584 | tf_op jit(solution)/shard_map/ppermute | solution.py:57
  26.7 2.0 %collective-permute-done.2 = f32[1,8,256]{2,1,0:T(8,128)S(1)} collective-permute-done((f32[1,8,256]{2,1,0:T(8,128)S(1)}, f32[1,8,256]{2,1,0:T(8,128)S(1)}, u32[]{:S(2)}, u32[]{:S(2)}) %collective-permute-start.2) | collective-permute-done | bytes 8224 | tf_op jit(solution)/shard_map/ppermute | solution.py:57
  28.8 2.6 %collective-permute-start.3 = (f32[1,8,256]{2,1,0:T(8,128)S(1)}, f32[1,8,256]{2,1,0:T(8,128)S(1)}, u32[]{:S(2)}, u32[]{:S(2)}) collective-permute-start(f32[1,8,256]{2,1,0:T(8,128)S(1)} %bitcast_add_fusion.4), channel_id=1, source_target_pairs={{0,2},{1,3},{2,0},{3,1},{4,6},{5,7},{6,4},{7,5},{8,10},{9,11},{10,... | collective-permute-start | bytes 24584 | tf_op jit(solution)/shard_map/ppermute | solution.py:57
  31.3 2.0 %collective-permute-done.3 = f32[1,8,256]{2,1,0:T(8,128)S(1)} collective-permute-done((f32[1,8,256]{2,1,0:T(8,128)S(1)}, f32[1,8,256]{2,1,0:T(8,128)S(1)}, u32[]{:S(2)}, u32[]{:S(2)}) %collective-permute-start.3) | collective-permute-done | bytes 8224 | tf_op jit(solution)/shard_map/ppermute | solution.py:57
  33.5 1.1 fusion.47
  34.9 1.0 fusion.11
  37.1 1.5 %slice_bitcast_fusion = (bf16[33,2,16,256]{3,0,2,1:T(8,128)(2,1)}, bf16[33,2,16,256]{3,0,2,1:T(8,128)(2,1)}) fusion(bf16[1,33,2,16,256]{4,1,3,2,0:T(8,128)(2,1)S(1)} %fusion.11), kind=kLoop, calls=%fused_computation.59 | loop fusion | bytes 1622016 | tf_op jit(solution)/shard_map/reshape.61
  38.6 1.3 %fusion.53 = f32[33,2,16,256]{3,2,1,0:T(8,128)} fusion(bf16[33,2,16,256]{3,0,2,1:T(8,128)(2,1)S(1)} %bitcast.311, bf16[3,256,256]{2,1,0:T(8,128)(2,1)S(1)} %copy-done.8), kind=kOutput, calls=%fused_computation.99 | convolution fusion | flops 138412032 | bytes 1867776 | tf_op jit(solution)/shard_map/nfhwd,cd->nfhwc/dot_general | solution.py:167
  40.0 1.4 %concatenate.21 = f32[2,2,2,2,2,6144]{5,4,3,2,1,0:T(2,128)} reshape(f32[3,256,256]{2,1,0:T(8,128)S(1)} %pad_maximum_fusion) | data formatting | bytes 1572864 | tf_op jit(solution)/shard_map/concatenate | solution.py:183
  41.4 2.0 %convolution_add_fusion.1 = f32[33,2,16,256]{3,2,1,0:T(8,128)S(1)} fusion(f32[33,2,16,256]{3,2,1,0:T(8,128)} %fusion.53, bf16[33,2,16,256]{3,0,2,1:T(8,128)(2,1)} %get-tuple-element.4, bf16[3,256,256]{2,1,0:T(8,128)(2,1)} %param.11), kind=kOutput, calls=%fused_computation.14 | convolution fusion | flops 138682368 | bytes 2949120 | tf_op jit(solution)/shard_map/nfhwd,cd->nfhwc/dot_general | solution.py:167
  43.4 1.5 %fusion.12 = bf16[33,2,16,256]{3,2,1,0:T(8,128)(2,1)S(1)} fusion(f32[33,2,16,256]{3,2,1,0:T(8,128)S(1)} %convolution_add_fusion.1, f32[33,2,16,256]{3,2,1,0:T(8,128)S(1)} %copy-done.14, bf16[33,2,16,256]{3,0,2,1:T(8,128)(2,1)S(1)} %copy-done.11, bf16[3,256,256]{2,1,0:T(8,128)(2,1)} %param.11), kind=kOutput, calls=%fused_computation.30 | convolution fusion | flops 141115392 | bytes 3375104 | tf_op jit(solution)/shard_map/nfhwd,cd->nfhwc/dot_general | solution.py:167
  44.9 1.1 fusion.23
  46.0 1.1 fusion.22
  47.1 1.1 fusion.21
  48.2 1.1 fusion.20
  49.3 1.1 fusion.19
  50.4 1.1 fusion.18
  51.5 1.1 fusion.17
  52.6 1.1 fusion.16
  53.7 1.3 %fusion.15 = f32[9,256,256]{2,1,0:T(8,128)} fusion(f32[9,256,256]{2,1,0:T(8,128)} %fusion.16, bf16[33,2,16,256]{3,2,1,0:T(8,128)(2,1)S(1)} %fusion.12, bf16[1,33,4,18,256]{4,3,2,1,0:T(8,128)(2,1)S(1)} %fusion.5), kind=kOutput, calls=%fused_computation.37 | convolution fusion | flops 138412032 | bytes 1343488 | tf_op jit(solution)/shard_map/nfhwc,nfhwd->cd/dot_general | solution.py:179
  55.0 4.0 %concatenate.20 = f32[2,2,2,2,2,18432]{5,4,3,2,1,0:T(2,128)} reshape(f32[9,256,256]{2,1,0:T(8,128)} %fusion.15) | data formatting | bytes 4718592 | tf_op jit(solution)/shard_map/concatenate | solution.py:183
  59.0 2.0 %constant_dynamic-update-slice_fusion.1 = f32[2,2,2,2,2,24576]{5,4,3,2,1,0:T(2,128)S(1)} fusion(f32[2,2,2,2,2,18432]{5,4,3,2,1,0:T(2,128)} %concatenate.20), kind=kLoop, calls=%fused_computation.141 | loop fusion | bytes 4718592
  61.1 1.3 %dynamic-slice_bitcast_fusion = f32[2,2,2,2,24576]{4,2,3,0,1:T(2,128)} fusion(f32[2,2,2,2,2,24576]{5,4,3,2,1,0:T(2,128)S(1)} %constant_dynamic-update-slice_fusion, s32[]{:T(128)S(6)} %select_n.86), kind=kLoop, calls=%fused_computation.10 | loop fusion | bytes 3145732 | tf_op jit(solution)/shard_map/jit(dynamic_index_in_dim)/squeeze | solution.py:78
  62.4 3.7 %collective-permute-done.4 = f32[2,2,2,2,24576]{4,2,3,0,1:T(2,128)} collective-permute-done((f32[2,2,2,2,24576]{4,2,3,0,1:T(2,128)}, f32[2,2,2,2,24576]{4,2,3,0,1:T(2,128)}, u32[]{:S(2)}, u32[]{:S(2)}) %collective-permute-start.4) | collective-permute-done | bytes 1572896 | tf_op jit(solution)/shard_map/ppermute | solution.py:79
  66.1 2.2 %bitcast_add_fusion = f32[2,2,2,2,24576]{4,2,3,0,1:T(2,128)S(1)} fusion(f32[2,2,2,2,24576]{4,2,3,0,1:T(2,128)} %collective-permute-done.4, f32[2,2,2,2,2,24576]{5,4,3,2,1,0:T(2,128)S(1)} %constant_dynamic-update-slice_fusion, s32[]{:T(128)S(6)} %select_n.85), kind=kLoop, calls=%fused_computation.9 | loop fusion | flops 393216 | bytes 4718596 | tf_op jit(solution)/shard_map/add | solution.py:79
  68.3 1.1 copy-done.1
  69.6 1.5 %collective-permute-start.5 = (f32[2,2,2,24576]{3,1,2,0:T(2,128)S(1)}, f32[2,2,2,24576]{3,1,2,0:T(2,128)S(1)}, u32[]{:S(2)}, u32[]{:S(2)}) collective-permute-start(f32[2,2,2,24576]{3,1,2,0:T(2,128)S(1)} %dynamic-slice_bitcast_fusion.1), channel_id=1, source_target_pairs={{0,8},{4,12},{8,0},{12,4},{16,24},{20,28},{24,16},{28,20},{1,9},{5... | collective-permute-start | bytes 2359304 | tf_op jit(solution)/shard_map/ppermute | solution.py:79
  71.1 18.1 %collective-permute-done.5 = f32[2,2,2,24576]{3,1,2,0:T(2,128)S(1)} collective-permute-done((f32[2,2,2,24576]{3,1,2,0:T(2,128)S(1)}, f32[2,2,2,24576]{3,1,2,0:T(2,128)S(1)}, u32[]{:S(2)}, u32[]{:S(2)}) %collective-permute-start.5) | collective-permute-done | bytes 786464 | tf_op jit(solution)/shard_map/ppermute | solution.py:79
  89.2 1.5 %bitcast_add_fusion.1 = f32[2,2,2,24576]{3,1,2,0:T(2,128)S(1)} fusion(f32[2,2,2,24576]{3,1,2,0:T(2,128)S(1)} %collective-permute-done.5, f32[2,2,2,2,24576]{4,2,3,0,1:T(2,128)} %copy-done.1, s32[]{:T(128)S(6)} %select_n.89), kind=kLoop, calls=%fused_computation.57 | loop fusion | flops 196608 | bytes 2359300 | tf_op jit(solution)/shard_map/add | solution.py:79
  90.8 1.6 %collective-permute-start.6 = (f32[2,2,24576]{2,0,1:T(2,128)S(1)}, f32[2,2,24576]{2,0,1:T(2,128)S(1)}, u32[]{:S(2)}, u32[]{:S(2)}) collective-permute-start(f32[2,2,24576]{2,0,1:T(2,128)S(1)} %dynamic-slice_bitcast_fusion.2), channel_id=1, source_target_pairs={{0,16},{4,20},{8,24},{12,28},{16,0},{20,4},{24,8},{28,12},{1,17},{... | collective-permute-start | bytes 1179656 | tf_op jit(solution)/shard_map/ppermute | solution.py:79
  92.3 8.8 %collective-permute-done.6 = f32[2,2,24576]{2,0,1:T(2,128)S(1)} collective-permute-done((f32[2,2,24576]{2,0,1:T(2,128)S(1)}, f32[2,2,24576]{2,0,1:T(2,128)S(1)}, u32[]{:S(2)}, u32[]{:S(2)}) %collective-permute-start.6) | collective-permute-done | bytes 393248 | tf_op jit(solution)/shard_map/ppermute | solution.py:79
  101.9 1.7 %collective-permute-start.7 = (f32[2,24576]{1,0:T(2,128)S(1)}, f32[2,24576]{1,0:T(2,128)S(1)}, u32[]{:S(2)}, u32[]{:S(2)}) collective-permute-start(f32[2,24576]{1,0:T(2,128)S(1)} %bitcast.317), channel_id=1, source_target_pairs={{0,1},{1,0},{2,3},{3,2},{4,5},{5,4},{6,7},{7,6},{8,9},{9,8},{10,11... | collective-permute-start | bytes 589832 | tf_op jit(solution)/shard_map/ppermute | solution.py:79
  103.5 4.1 %collective-permute-done.7 = f32[2,24576]{1,0:T(2,128)S(1)} collective-permute-done((f32[2,24576]{1,0:T(2,128)S(1)}, f32[2,24576]{1,0:T(2,128)S(1)}, u32[]{:S(2)}, u32[]{:S(2)}) %collective-permute-start.7) | collective-permute-done | bytes 196640 | tf_op jit(solution)/shard_map/ppermute | solution.py:79
  108.0 2.6 %collective-permute-start.8 = (f32[24576]{0:T(1024)S(1)}, f32[24576]{0:T(1024)S(1)}, u32[]{:S(2)}, u32[]{:S(2)}) collective-permute-start(f32[24576]{0:T(1024)S(1)} %bitcast.321), channel_id=1, source_target_pairs={{0,2},{1,3},{2,0},{3,1},{4,6},{5,7},{6,4},{7,5},{8,10},{9,11},{10,... | collective-permute-start | bytes 294920 | tf_op jit(solution)/shard_map/ppermute | solution.py:79
  110.6 3.0 %collective-permute-done.8 = f32[24576]{0:T(1024)S(1)} collective-permute-done((f32[24576]{0:T(1024)S(1)}, f32[24576]{0:T(1024)S(1)}, u32[]{:S(2)}, u32[]{:S(2)}) %collective-permute-start.8) | collective-permute-done | bytes 98336 | tf_op jit(solution)/shard_map/ppermute | solution.py:79
  (71 shorter events, 8.4 us)
Async XLA Ops:
  0.6 22.6 %copy-start = (bf16[256,256]{1,0:T(8,128)(2,1)S(1)}, bf16[256,256]{1,0:T(8,128)(2,1)}, u32[]{:S(2)}) copy-start(bf16[256,256]{1,0:T(8,128)(2,1)} %param.12) | copy-start | bytes 393220
  0.6 10.4 %collective-permute-start = (bf16[1,33,1,8,256]{4,3,2,1,0:T(8,128)(2,1)}, bf16[1,33,1,8,256]{4,3,2,1,0:T(8,128)(2,1)S(1)}, u32[]{:S(2)}, u32[]{:S(2)}) collective-permute-start(bf16[1,33,1,8,256]{4,3,2,1,0:T(8,128)(2,1)} %param.8), channel_id=1, source_target_pairs={{0,1},{1,2},{2,3},{4,5},{5,6},{6,7},{8,9},{9,10},{10,11},{12,13},{... | collective-permute-start | bytes 405512 | tf_op jit(solution)/shard_map/ppermute | solution.py:19
  5.8 7.2 %collective-permute-start.1 = (bf16[1,33,1,8,256]{4,3,2,1,0:T(8,128)(2,1)}, bf16[1,33,1,8,256]{4,3,2,1,0:T(8,128)(2,1)S(1)}, u32[]{:S(2)}, u32[]{:S(2)}) collective-permute-start(bf16[1,33,1,8,256]{4,3,2,1,0:T(8,128)(2,1)} %param.8), channel_id=1, source_target_pairs={{1,0},{2,1},{3,2},{5,4},{6,5},{7,6},{9,8},{10,9},{11,10},{13,12},{... | collective-permute-start | bytes 405512 | tf_op jit(solution)/shard_map/ppermute | solution.py:20
  11.4 3.5 %copy-start.5 = (bf16[1,33,1,16,256]{4,3,2,1,0:T(8,128)(2,1)}, bf16[1,33,1,16,256]{4,3,2,1,0:T(8,128)(2,1)S(1)}, u32[]{:S(2)}) copy-start(bf16[1,33,1,16,256]{4,3,2,1,0:T(8,128)(2,1)S(1)} %slice.104) | copy-start | bytes 811012
  13.2 3.6 %copy-start.3 = (bf16[1,33,1,16,256]{4,3,2,1,0:T(8,128)(2,1)}, bf16[1,33,1,16,256]{4,3,2,1,0:T(8,128)(2,1)S(1)}, u32[]{:S(2)}) copy-start(bf16[1,33,1,16,256]{4,3,2,1,0:T(8,128)(2,1)S(1)} %slice.105) | copy-start | bytes 811012
  13.2 1.3 %copy-start.9 = (bf16[3,3,256,256]{3,2,1,0:T(8,128)(2,1)S(1)}, bf16[3,3,256,256]{3,2,1,0:T(8,128)(2,1)}, u32[]{:S(2)}) copy-start(bf16[3,3,256,256]{3,2,1,0:T(8,128)(2,1)} %param.10) | copy-start | bytes 3538948
  17.1 1.4 %copy-start.8 = (bf16[3,256,256]{2,1,0:T(8,128)(2,1)S(1)}, bf16[3,256,256]{2,1,0:T(8,128)(2,1)}, u32[]{:S(2)}) copy-start(bf16[3,256,256]{2,1,0:T(8,128)(2,1)} %param.11) | copy-start | bytes 1179652
  18.8 1.1 copy-start.7
  19.9 6.8 %copy-start.12 = (f32[256]{0:T(256)S(1)}, f32[256]{0:T(256)}, u32[]{:S(2)}) copy-start(f32[256]{0:T(256)} %param.13) | copy-start | bytes 3076
  21.0 13.9 %copy-start.13 = (s32[1,8]{1,0:T(1,128)S(1)}, s32[1,8]{1,0:T(1,128)}, u32[]{:S(2)}) copy-start(s32[1,8]{1,0:T(1,128)} %param.14) | copy-start | bytes 100
  25.1 3.7 %collective-permute-start.2 = (f32[1,8,256]{2,1,0:T(8,128)S(1)}, f32[1,8,256]{2,1,0:T(8,128)S(1)}, u32[]{:S(2)}, u32[]{:S(2)}) collective-permute-start(f32[1,8,256]{2,1,0:T(8,128)S(1)} %bitcast.322), channel_id=1, source_target_pairs={{0,1},{1,0},{2,3},{3,2},{4,5},{5,4},{6,7},{7,6},{8,9},{9,8},{10,11... | collective-permute-start | bytes 24584 | tf_op jit(solution)/shard_map/ppermute | solution.py:57
  28.8 4.5 %collective-permute-start.3 = (f32[1,8,256]{2,1,0:T(8,128)S(1)}, f32[1,8,256]{2,1,0:T(8,128)S(1)}, u32[]{:S(2)}, u32[]{:S(2)}) collective-permute-start(f32[1,8,256]{2,1,0:T(8,128)S(1)} %bitcast_add_fusion.4), channel_id=1, source_target_pairs={{0,2},{1,3},{2,0},{3,1},{4,6},{5,7},{6,4},{7,5},{8,10},{9,11},{10,... | collective-permute-start | bytes 24584 | tf_op jit(solution)/shard_map/ppermute | solution.py:57
  31.3 3.6 %copy-start.10 = (bf16[1,33,2,16,256]{4,3,2,1,0:T(8,128)(2,1)S(1)}, bf16[1,33,2,16,256]{4,3,2,1,0:T(8,128)(2,1)}, u32[]{:S(2)}) copy-start(bf16[1,33,2,16,256]{4,3,2,1,0:T(8,128)(2,1)} %param.15) | copy-start | bytes 1622020
  41.4 2.0 %copy-start.11 = (bf16[33,2,16,256]{3,0,2,1:T(8,128)(2,1)S(1)}, bf16[33,2,16,256]{3,0,2,1:T(8,128)(2,1)}, u32[]{:S(2)}) copy-start(bf16[33,2,16,256]{3,0,2,1:T(8,128)(2,1)} %get-tuple-element.3) | copy-start | bytes 1622020
  41.4 2.0 %copy-start.14 = (f32[33,2,16,256]{3,2,1,0:T(8,128)S(1)}, f32[33,2,16,256]{3,2,1,0:T(8,128)}, u32[]{:S(2)}) copy-start(f32[33,2,16,256]{3,2,1,0:T(8,128)} %get-tuple-element.12) | copy-start | bytes 3244036
  44.9 1.1 copy-start.6
  51.5 1.1 copy-start.4
  59.0 2.0 %copy-start.2 = (f32[2,2,2,2,2,6144]{5,4,3,2,1,0:T(2,128)S(1)}, f32[2,2,2,2,2,6144]{5,4,3,2,1,0:T(2,128)}, u32[]{:S(2)}) copy-start(f32[2,2,2,2,2,6144]{5,4,3,2,1,0:T(2,128)} %concatenate.21) | copy-start | bytes 2359300
  62.4 3.8 %collective-permute-start.4 = (f32[2,2,2,2,24576]{4,2,3,0,1:T(2,128)}, f32[2,2,2,2,24576]{4,2,3,0,1:T(2,128)}, u32[]{:S(2)}, u32[]{:S(2)}) collective-permute-start(f32[2,2,2,2,24576]{4,2,3,0,1:T(2,128)} %dynamic-slice_bitcast_fusion), channel_id=1, source_target_pairs={{0,4},{4,0},{8,12},{12,8},{16,20},{20,16},{24,28},{28,24},{1,5},{5... | collective-permute-start | bytes 4718600 | tf_op jit(solution)/shard_map/ppermute | solution.py:79
  68.3 1.2 %copy-start.1 = (f32[2,2,2,2,24576]{4,2,3,0,1:T(2,128)}, f32[2,2,2,2,24576]{4,2,3,0,1:T(2,128)S(1)}, u32[]{:S(2)}) copy-start(f32[2,2,2,2,24576]{4,2,3,0,1:T(2,128)S(1)} %bitcast_add_fusion) | copy-start | bytes 4718596
  69.6 19.6 %collective-permute-start.5 = (f32[2,2,2,24576]{3,1,2,0:T(2,128)S(1)}, f32[2,2,2,24576]{3,1,2,0:T(2,128)S(1)}, u32[]{:S(2)}, u32[]{:S(2)}) collective-permute-start(f32[2,2,2,24576]{3,1,2,0:T(2,128)S(1)} %dynamic-slice_bitcast_fusion.1), channel_id=1, source_target_pairs={{0,8},{4,12},{8,0},{12,4},{16,24},{20,28},{24,16},{28,20},{1,9},{5... | collective-permute-start | bytes 2359304 | tf_op jit(solution)/shard_map/ppermute | solution.py:79
  90.8 10.4 %collective-permute-start.6 = (f32[2,2,24576]{2,0,1:T(2,128)S(1)}, f32[2,2,24576]{2,0,1:T(2,128)S(1)}, u32[]{:S(2)}, u32[]{:S(2)}) collective-permute-start(f32[2,2,24576]{2,0,1:T(2,128)S(1)} %dynamic-slice_bitcast_fusion.2), channel_id=1, source_target_pairs={{0,16},{4,20},{8,24},{12,28},{16,0},{20,4},{24,8},{28,12},{1,17},{... | collective-permute-start | bytes 1179656 | tf_op jit(solution)/shard_map/ppermute | solution.py:79
  101.9 5.7 %collective-permute-start.7 = (f32[2,24576]{1,0:T(2,128)S(1)}, f32[2,24576]{1,0:T(2,128)S(1)}, u32[]{:S(2)}, u32[]{:S(2)}) collective-permute-start(f32[2,24576]{1,0:T(2,128)S(1)} %bitcast.317), channel_id=1, source_target_pairs={{0,1},{1,0},{2,3},{3,2},{4,5},{5,4},{6,7},{7,6},{8,9},{9,8},{10,11... | collective-permute-start | bytes 589832 | tf_op jit(solution)/shard_map/ppermute | solution.py:79
  108.0 5.6 %collective-permute-start.8 = (f32[24576]{0:T(1024)S(1)}, f32[24576]{0:T(1024)S(1)}, u32[]{:S(2)}, u32[]{:S(2)}) collective-permute-start(f32[24576]{0:T(1024)S(1)} %bitcast.321), channel_id=1, source_target_pairs={{0,2},{1,3},{2,0},{3,1},{4,6},{5,7},{6,4},{7,5},{8,10},{9,11},{10,... | collective-permute-start | bytes 294920 | tf_op jit(solution)/shard_map/ppermute | solution.py:79
